TPU v7x, 256 devices: a whole 4x4x8 slice. The times are simulated.
256 devices in a mesh: row: 16 (over y_lo, x, core), col: 16 (over y_hi, z).
Axes of the slice: x: 4, y: 4 (y_hi: 2, y_lo: 2; y = y_hi * 2 + y_lo), z: 8, core: 2. Of those that a mesh axis runs over, the one named last changes fastest.
Arguments:
- tiles: bfloat16 [16, 16, 128, 128, 128], P('row', 'col'), as said below
- coords: int32 [16, 16, 2, 128], P('row', 'col'), may hold values from 0 to 63, as said below
- counts: int32 [16, 16], P('row', 'col'), may hold values from 1 to 128, as said below
- valid: int32 [131072], P(('row', 'col')), may hold values 0 or 1
- start: float32 [8, 131072], P(None, ('row', 'col'))
- rotations: float32 [2, 8, 24], replicated, as said below
Outputs:
- eigenmaps: float32 [8, 131072], P(None, ('row', 'col'))
- ritz: float32 [8, 8], replicated
Inputs may be any that keep to these rules, and one draw needn't show every extreme that they name: coords[r, c, 0, s] is a block row from 0 to 63 and coords[r, c, 1, s] a block column from 0 to 63; the live slots of one owner name distinct blocks, each on or above the block diagonal (g_row <= g_col). The live slots of an owner are the first counts[r, c] of its list; one owner in grid row 0 has all 128 live. `tiles`: nonnegative; a tile on the block diagonal is symmetric. The Rayleigh-Ritz coefficients of the current vectors, rotations[t, :, 0 to 7], form a matrix whose diagonal dominates its rows.
All inputs are finite; a program needn't handle non-finite values. No bound on the sum of `valid` on one device may be relied on, other than what follows from the above.
Results may differ from a plain program's by a relative error of at most 0.0013.
Values may be sent and summed in bfloat16 or wider, within the bound.
No kernel may reach another device: no remote copies, remote signals or barrier semaphores. Data moves between devices by JAX's collectives and lax.ppermute only.
A program may use at most 64 MiB of HBM per device.

v0:
```python
import jax
import jax.numpy as jnp
from jax import lax
from jax.sharding import PartitionSpec as P


def matmul_high(left, right):
    return jnp.dot(left, right, precision=lax.Precision.HIGHEST)


def lower_inverse(lower_factor):
    order_size = lower_factor.shape[0]
    identity = jnp.eye(order_size, dtype=lower_factor.dtype)
    inverse_rows = []
    for row_at in range(order_size):
        partial_row = identity[row_at]
        for prior_at in range(row_at):
            partial_row = partial_row - lower_factor[row_at, prior_at] * inverse_rows[prior_at]
        inverse_rows.append(partial_row / lower_factor[row_at, row_at])
    return jnp.stack(inverse_rows)


def settle(new_vecs, new_images, new_steps, step_images, gram_x, gram_ax, node_total):
    lower_factor = jnp.linalg.cholesky(gram_x / node_total)
    inverse = lower_inverse(lower_factor)
    theta = matmul_high(matmul_high(inverse, gram_ax / node_total), inverse.T)
    return (
        matmul_high(inverse, new_vecs),
        matmul_high(inverse, new_images),
        matmul_high(inverse, new_steps),
        matmul_high(inverse, step_images),
        theta,
    )


def gram_sums(new_vecs, new_images):
    return lax.psum(
        (matmul_high(new_vecs, new_vecs.T), matmul_high(new_images, new_vecs.T)), ("row", "col")
    )


def local_terms(
    part_tiles, part_rows, part_cols, weight_direct, weight_mirror, col_blocks, row_blocks
):
    row_span = row_blocks.shape[1]
    col_span = col_blocks.shape[1]
    col_values = jnp.take(col_blocks, part_cols, axis=1)
    row_values = jnp.take(row_blocks, part_rows, axis=1)
    direct = (
        jnp.einsum("sut,cst->csu", part_tiles, col_values, preferred_element_type=jnp.float32)
        * weight_direct[None, :, None]
    )
    mirror = (
        jnp.einsum("sut,csu->cst", part_tiles, row_values, preferred_element_type=jnp.float32)
        * weight_mirror[None, :, None]
    )
    pick_rows = (part_rows[:, None] == jnp.arange(row_span, dtype=jnp.int32)[None, :]).astype(
        jnp.float32
    )
    pick_cols = (part_cols[:, None] == jnp.arange(col_span, dtype=jnp.int32)[None, :]).astype(
        jnp.float32
    )
    rows_sum = jnp.einsum("sp,csu->cpu", pick_rows, direct, precision=lax.Precision.HIGHEST)
    cols_sum = jnp.einsum("sq,cst->cqt", pick_cols, mirror, precision=lax.Precision.HIGHEST)
    return (rows_sum, cols_sum)


def body(tiles, coords, counts, valid, start, rotations):
    row_count = lax.axis_size("row")
    col_count = lax.axis_size("col")
    row_index = lax.axis_index("row")
    col_index = lax.axis_index("col")
    slot_count = tiles.shape[2]
    tile_side = tiles.shape[3]
    stretch_nodes = valid.shape[0]
    per_stretch = stretch_nodes // tile_side
    row_span = col_count * per_stretch
    col_span = row_count * per_stretch
    node_total = jnp.float32(stretch_nodes * row_count * col_count)
    vec_count = start.shape[0]
    flat_tiles = tiles.reshape(slot_count, tile_side, tile_side)
    block_rows = coords[0, 0, 0]
    block_cols = coords[0, 0, 1]
    live_count = counts[0, 0]
    global_rows = row_index * row_span + block_rows
    global_cols = (
        block_cols // per_stretch * col_count + col_index
    ) * per_stretch + block_cols % per_stretch
    live = (jnp.arange(slot_count, dtype=jnp.int32) < live_count).astype(jnp.float32)
    mirror_weight = live * (global_rows != global_cols).astype(jnp.float32)

    def graph_product(vectors):
        width = vectors.shape[0]
        short = vectors.astype(jnp.bfloat16)
        col_side = lax.all_gather(short, "row", axis=1, tiled=True)
        row_side = lax.all_gather(short, "col", axis=1, tiled=True)
        col_blocks = col_side.reshape(width, col_span, tile_side)
        row_blocks = row_side.reshape(width, row_span, tile_side)
        rows_total, cols_total = local_terms(
            flat_tiles, block_rows, block_cols, live, mirror_weight, col_blocks, row_blocks
        )
        direct_part = lax.psum_scatter(
            rows_total.reshape(width, row_span * tile_side), "col", scatter_dimension=1, tiled=True
        )
        mirror_part = lax.psum_scatter(
            cols_total.reshape(width, col_span * tile_side), "row", scatter_dimension=1, tiled=True
        )
        return direct_part + mirror_part

    node_mask = valid.astype(jnp.float32)
    first_vecs = start * node_mask[None, :]
    raw = graph_product(jnp.concatenate([node_mask[None, :], first_vecs], 0))
    degree = raw[0]
    first_images = node_mask[None, :] * (degree[None, :] * first_vecs - raw[1:])
    zero_steps = jnp.zeros_like(first_vecs)
    gram_x, gram_ax = gram_sums(first_vecs, first_images)
    vecs, images, steps, step_images, theta = settle(
        first_vecs, first_images, zero_steps, zero_steps, gram_x, gram_ax, node_total
    )
    for turn in range(rotations.shape[0]):
        resid = images - matmul_high(theta, vecs)
        resid_images = node_mask[None, :] * (degree[None, :] * resid - graph_product(resid))
        stacked = jnp.concatenate([vecs, resid, steps], 0)
        stacked_images = jnp.concatenate([images, resid_images, step_images], 0)
        rotation = rotations[turn]
        new_vecs = matmul_high(rotation, stacked)
        new_images = matmul_high(rotation, stacked_images)
        gram_x, gram_ax = gram_sums(new_vecs, new_images)
        new_steps = matmul_high(rotation[:, vec_count:], stacked[vec_count:])
        new_step_images = matmul_high(rotation[:, vec_count:], stacked_images[vec_count:])
        vecs, images, steps, step_images, theta = settle(
            new_vecs, new_images, new_steps, new_step_images, gram_x, gram_ax, node_total
        )
    return (vecs, theta)


def solution(mesh):
    in_specs = (
        P("row", "col", None, None, None),
        P("row", "col", None, None),
        P("row", "col"),
        P(("row", "col")),
        P(None, ("row", "col")),
        P(),
    )
    out_specs = (P(None, ("row", "col")), P())
    return jax.shard_map(body, mesh=mesh, in_specs=in_specs, out_specs=out_specs, check_vma=False)
```

profile of v0, /device:TPU:1, one launch (start us, length us, event | category | flops | bytes accessed | tf_op | source)
XLA Modules:
  0.0 1272.5 jit_solution(13226586753436208169)
XLA Ops:
  10.2 39.4 %all_gather.19 = bf16[9,8192]{1,0:T(8,128)(2,1)S(1)} all-gather(bf16[9,512]{1,0:T(8,128)(2,1)S(1)} %pad_maximum_fusion.8), channel_id=1, replica_groups=mesh['row'=16,'col'=16] {'col'}, dimensions={1}, use_global_device_ids=true | all-gather | bytes 156672 | tf_op jit(solution)/shard_map/all_gather | solution.py:96
  51.2 3.4 fusion.8
  56.4 26.8 %all_gather.18 = bf16[9,8192]{1,0:T(8,128)(2,1)S(1)} all-gather(bf16[9,512]{1,0:T(8,128)(2,1)S(1)} %pad_maximum_fusion.8), channel_id=1, replica_groups=mesh['row'=16,'col'=16] {'row'}, dimensions={1}, use_global_device_ids=true | all-gather | bytes 156672 | tf_op jit(solution)/shard_map/all_gather | solution.py:95
  84.2 4.5 fusion.10
  90.7 26.8 %reduce-scatter.9.cloned.1.call-done = f32[9,512]{1,0:T(8,128)} async-done(((f32[9,8192]{1,0:T(8,128)}), f32[9,512]{1,0:T(8,128)}) %reduce-scatter.9.cloned.1.call-update) | async-done | bytes 18448 | tf_op jit(solution)/shard_map/reduce_scatter | solution.py:105
  117.5 198.7 %reduce-scatter.7.cloned.1.call-done = f32[9,512]{1,0:T(8,128)} async-done(((f32[9,8192]{1,0:T(8,128)}), f32[9,512]{1,0:T(8,128)}) %reduce-scatter.7.cloned.1.call-update) | async-done | bytes 18448 | tf_op jit(solution)/shard_map/reduce_scatter | solution.py:102
  317.1 79.7 %all-reduce.2 = (f32[8,8]{0,1:T(8,128)S(1)}, f32[8,8]{0,1:T(8,128)S(1)}) all-reduce(f32[8,8]{0,1:T(8,128)S(1)} %fusion.95, f32[8,8]{0,1:T(8,128)S(1)} %fusion.87), channel_id=1, replica_groups=mesh['row'=16,'col'=16] {'row','col'}, use_global_device_ids=true, to_apply=%region_0.1 | all-reduce | flops 128 | bytes 1024 | tf_op jit(solution)/shard_map/psum | solution.py:37
  400.4 22.6 %subtract_divide_fusion.14 = (f32[1,8]{1,0:T(1,128)S(1)}, f32[1,8]{1,0:T(1,128)S(1)}, f32[1,8]{1,0:T(1,128)S(1)}, f32[1,8]{1,0:T(1,128)S(1)}, f32[1,8]{1,0:T(1,1...) fusion(f32[]{:T(128)} %bitcast.36, f32[]{:T(128)} %bitcast.35, f32[]{:T(128)} %bitcast.34, ...), kind=kLoop, calls=%fused_computation.199 | loop fusion | flops 512 | bytes 656 | tf_op jit(solution)/shard_map/div | solution.py:19
  423.7 31.8 %all_gather.21 = bf16[8,8192]{1,0:T(8,128)(2,1)S(1)} all-gather(bf16[8,512]{1,0:T(8,128)(2,1)S(1)} %get-tuple-element.153), channel_id=1, replica_groups=mesh['row'=16,'col'=16] {'col'}, dimensions={1}, use_global_device_ids=true | all-gather | bytes 139264 | tf_op jit(solution)/shard_map/all_gather | solution.py:96
  455.4 24.9 %all_gather.20 = bf16[8,8192]{1,0:T(8,128)(2,1)S(1)} all-gather(bf16[8,512]{1,0:T(8,128)(2,1)S(1)} %get-tuple-element.153), channel_id=1, replica_groups=mesh['row'=16,'col'=16] {'row'}, dimensions={1}, use_global_device_ids=true | all-gather | bytes 139264 | tf_op jit(solution)/shard_map/all_gather | solution.py:95
  481.1 3.4 fusion.4
  486.6 4.5 fusion.6
  493.5 45.7 %reduce-scatter.13.cloned.1.call-done = f32[8,512]{1,0:T(8,128)} async-done(((f32[8,8192]{1,0:T(8,128)}), f32[8,512]{1,0:T(8,128)}) %reduce-scatter.13.cloned.1.call-update) | async-done | bytes 16400 | tf_op jit(solution)/shard_map/reduce_scatter | solution.py:105
  539.2 197.1 %reduce-scatter.11.cloned.1.call-done = f32[8,512]{1,0:T(8,128)} async-done(((f32[8,8192]{1,0:T(8,128)}), f32[8,512]{1,0:T(8,128)}) %reduce-scatter.11.cloned.1.call-update) | async-done | bytes 16400 | tf_op jit(solution)/shard_map/reduce_scatter | solution.py:102
  737.3 79.8 %all-reduce.1 = (f32[8,8]{0,1:T(8,128)S(1)}, f32[8,8]{0,1:T(8,128)S(1)}) all-reduce(f32[8,8]{0,1:T(8,128)S(1)} %fusion.152, f32[8,8]{0,1:T(8,128)S(1)} %fusion.155), channel_id=1, replica_groups=mesh['row'=16,'col'=16] {'row','col'}, use_global_device_ids=true, to_apply=%region_6.9 | all-reduce | flops 128 | bytes 1024 | tf_op jit(solution)/shard_map/psum | solution.py:37
  820.7 22.6 %subtract_divide_fusion.7 = (f32[1,8]{1,0:T(1,128)S(1)}, f32[1,8]{1,0:T(1,128)S(1)}, f32[1,8]{1,0:T(1,128)S(1)}, f32[1,8]{1,0:T(1,128)S(1)}, f32[1,8]{1,0:T(1,12...) fusion(f32[]{:T(128)} %bitcast.87, f32[]{:T(128)} %bitcast.86, f32[]{:T(128)} %bitcast.85, ...), kind=kLoop, calls=%fused_computation.190 | loop fusion | flops 512 | bytes 656 | tf_op jit(solution)/shard_map/div | solution.py:19
  844.0 31.8 %all_gather.23 = bf16[8,8192]{1,0:T(8,128)(2,1)S(1)} all-gather(bf16[8,512]{1,0:T(8,128)(2,1)S(1)} %get-tuple-element.155), channel_id=1, replica_groups=mesh['row'=16,'col'=16] {'col'}, dimensions={1}, use_global_device_ids=true | all-gather | bytes 139264 | tf_op jit(solution)/shard_map/all_gather | solution.py:96
  875.8 24.9 %all_gather.22 = bf16[8,8192]{1,0:T(8,128)(2,1)S(1)} all-gather(bf16[8,512]{1,0:T(8,128)(2,1)S(1)} %get-tuple-element.155), channel_id=1, replica_groups=mesh['row'=16,'col'=16] {'row'}, dimensions={1}, use_global_device_ids=true | all-gather | bytes 139264 | tf_op jit(solution)/shard_map/all_gather | solution.py:95
  901.4 3.4 fusion
  906.9 4.5 fusion.2
  914.3 45.1 %reduce-scatter.17.cloned.1.call-done = f32[8,512]{1,0:T(8,128)} async-done(((f32[8,8192]{1,0:T(8,128)}), f32[8,512]{1,0:T(8,128)}) %reduce-scatter.17.cloned.1.call-update) | async-done | bytes 16400 | tf_op jit(solution)/shard_map/reduce_scatter | solution.py:105
  959.4 197.2 %reduce-scatter.15.cloned.1.call-done = f32[8,512]{1,0:T(8,128)} async-done(((f32[8,8192]{1,0:T(8,128)}), f32[8,512]{1,0:T(8,128)}) %reduce-scatter.15.cloned.1.call-update) | async-done | bytes 16400 | tf_op jit(solution)/shard_map/reduce_scatter | solution.py:102
  1158.2 79.7 %all-reduce = (f32[8,8]{0,1:T(8,128)S(1)}, f32[8,8]{0,1:T(8,128)S(1)}) all-reduce(f32[8,8]{0,1:T(8,128)S(1)} %fusion.158, f32[8,8]{0,1:T(8,128)S(1)} %fusion.161), channel_id=1, replica_groups=mesh['row'=16,'col'=16] {'row','col'}, use_global_device_ids=true, to_apply=%region_10.14 | all-reduce | flops 128 | bytes 1024 | tf_op jit(solution)/shard_map/psum | solution.py:37
  1241.4 22.6 %subtract_divide_fusion = (f32[1,8]{1,0:T(1,128)S(1)}, f32[1,8]{1,0:T(1,128)S(1)}, f32[1,8]{1,0:T(1,128)S(1)}, f32[1,8]{1,0:T(1,128)S(1)}, f32[1,8]{1,0:T(1,128)...) fusion(f32[]{:T(128)} %bitcast.133, f32[]{:T(128)} %bitcast.132, f32[]{:T(128)} %bitcast.131, ...), kind=kLoop, calls=%fused_computation.183 | loop fusion | flops 512 | bytes 656 | tf_op jit(solution)/shard_map/div | solution.py:19
  (117 shorter events, 36.5 us)
Async XLA Ops:
  7.2 47.5 %copy-start.2 = (s32[1,1,2,128]{3,2,1,0:T(2,128)S(1)}, s32[1,1,2,128]{3,2,1,0:T(2,128)}, u32[]{:S(2)}) copy-start(s32[1,1,2,128]{3,2,1,0:T(2,128)} %param.12) | copy-start | bytes 3076
  7.2 110.3 %reduce-scatter.9.cloned.1.call-start = ((), (), s32[]{:S(2)}) async-start(), calls=%async_computation.7 | async-start | bytes 557056 | tf_op jit(solution)/shard_map/reduce_scatter | solution.py:105
  56.4 259.8 %reduce-scatter.7.cloned.1.call-start = ((), (), s32[]{:S(2)}) async-start(), calls=%async_computation.6 | async-start | bytes 557056 | tf_op jit(solution)/shard_map/reduce_scatter | solution.py:102
  84.2 6.3 copy-start.1
  84.2 6.4 copy-start
  90.4 448.7 %reduce-scatter.13.cloned.1.call-start = ((), (), s32[]{:S(2)}) async-start(), calls=%async_computation.9 | async-start | bytes 278528 | tf_op jit(solution)/shard_map/reduce_scatter | solution.py:105
  485.8 250.4 %reduce-scatter.11.cloned.1.call-start = ((), (), s32[]{:S(2)}) async-start(), calls=%async_computation.8 | async-start | bytes 278528 | tf_op jit(solution)/shard_map/reduce_scatter | solution.py:102
  492.5 466.9 %reduce-scatter.17.cloned.1.call-start = ((), (), s32[]{:S(2)}) async-start(), calls=%async_computation.11 | async-start | bytes 278528 | tf_op jit(solution)/shard_map/reduce_scatter | solution.py:105
  906.2 250.4 %reduce-scatter.15.cloned.1.call-start = ((), (), s32[]{:S(2)}) async-start(), calls=%async_computation.10 | async-start | bytes 278528 | tf_op jit(solution)/shard_map/reduce_scatter | solution.py:102
Sparse Core Ops, SparseCore 0:
  56.5 60.9 reduce-scatter.8
  121.8 194.3 reduce-scatter.6
  485.9 53.1 reduce-scatter.12
  543.3 192.9 reduce-scatter.10
  906.3 53.0 reduce-scatter.16
  963.5 193.0 reduce-scatter.14
where the time goes:
time: 1270 us
  waiting for transfers between devices  711 us (56%)
  blocking collectives  419 us (33%)
  other arithmetic  78.4 us (6%)
  matrix products  33.7 us (3%)
  local copies, waits for them, and re-layouts  15.6 us (1%)
  between operations  15.1 us (1%)
    reduce_scatter x3, waiting for transfers between devices, graph_product(): lax.psum_scatter(rows_total.reshape(width, row_span * tile_side), 'col',...  593 us
    psum x3, blocking collectives, gram_sums(): lax.psum((matmul_high(new_vecs, new_vecs.T), matmul_high(new_images, new_...  239 us
    reduce_scatter x3, waiting for transfers between devices, graph_product(): lax.psum_scatter(cols_total.reshape(width, col_span * tile_side), 'row',...  118 us
    all_gather x3, blocking collectives, graph_product(): row_side = lax.all_gather(short, 'col', axis=1, tiled=True)  103 us
    all_gather x3, blocking collectives, graph_product(): col_side = lax.all_gather(short, 'row', axis=1, tiled=True)  76.7 us
    div x3, other arithmetic, lower_inverse(): inverse_rows.append(partial_row / lower_factor[row_at, row_at])  67.8 us
  transfers between devices with their start and end apart: 6, of which 6 were waited for; matrix products, arithmetic and copies ran while one was open for 2% of the time, Pallas kernels for 0%

commit v1 on v0

--- a/solution.py
+++ b/solution.py
@@ -93,7 +93,8 @@
         width = vectors.shape[0]
         short = vectors.astype(jnp.bfloat16)
         col_side = lax.all_gather(short, "row", axis=1, tiled=True)
-        row_side = lax.all_gather(short, "col", axis=1, tiled=True)
+        stack = jnp.stack([short] * lax.axis_size("col"))
+        row_side = jnp.concatenate(lax.all_to_all(stack, "col", 0, 0), axis=1)
         col_blocks = col_side.reshape(width, col_span, tile_side)
         row_blocks = row_side.reshape(width, row_span, tile_side)
         rows_total, cols_total = local_terms(

time: 1270 us -> 1210 us (0.953)
  blocking collectives: 419 us -> 294 us
  waiting for transfers between devices: 711 us -> 749 us
  starting transfers between devices: 0.25 us -> 23.9 us
    all_gather x3 -> x0, blocking collectives: 103 us -> none  [graph_product(): row_side = lax.all_gather(short, 'col', axis=1, tiled=True)]
    reduce_scatter x3, waiting for transfers between devices: 118 us -> 196 us  [graph_product(): lax.psum_scatter(cols_total.reshape(width, col_span * tile_side), 'row',...]
    reduce_scatter x3, waiting for transfers between devices: 593 us -> 549 us  [graph_product(): lax.psum_scatter(rows_total.reshape(width, row_span * tile_side), 'col',...]
    all_to_all x0 -> x3, starting transfers between devices: none -> 23.7 us  [graph_product(): row_side = jnp.concatenate(lax.all_to_all(stack, 'col', 0, 0), axis=1)]
    all_gather x3, blocking collectives: 76.7 us -> 57.2 us  [graph_product(): col_side = lax.all_gather(short, 'row', axis=1, tiled=True)]
  transfers between devices with their start and end apart: 6 -> 9, of which waited for: 6 -> 8; matrix products, arithmetic and copies ran while one was open for 2% -> 3% of each run, Pallas kernels for 0% -> 0%
where the time goes in v1:
time: 1210 us
  waiting for transfers between devices  749 us (62%)
  blocking collectives  294 us (24%)
  other arithmetic  78.2 us (6%)
  matrix products  31.6 us (3%)
  starting transfers between devices  23.9 us (2%)
  local copies, waits for them, and re-layouts  17.8 us (1%)
  between operations  15.1 us (1%)
    reduce_scatter x3, waiting for transfers between devices, graph_product(): lax.psum_scatter(rows_total.reshape(width, row_span * tile_side), 'col',...  549 us
    psum x3, blocking collectives, gram_sums(): lax.psum((matmul_high(new_vecs, new_vecs.T), matmul_high(new_images, new_...  237 us
    reduce_scatter x3, waiting for transfers between devices, graph_product(): lax.psum_scatter(cols_total.reshape(width, col_span * tile_side), 'row',...  196 us
    div x3, other arithmetic, lower_inverse(): inverse_rows.append(partial_row / lower_factor[row_at, row_at])  67.6 us
    all_gather x3, blocking collectives, graph_product(): col_side = lax.all_gather(short, 'row', axis=1, tiled=True)  57.2 us
  transfers between devices with their start and end apart: 9, of which 8 were waited for; matrix products, arithmetic and copies ran while one was open for 3% of the time, Pallas kernels for 0%

profile of v1, /device:TPU:1, one launch (start us, length us, event | category | flops | bytes accessed | tf_op | source)
XLA Modules:
  0.0 1209.9 jit_solution(12387252787781038003)
XLA Ops:
  9.3 11.7 all-to-all-start
  22.6 20.3 %all_gather.9 = bf16[9,8192]{1,0:T(8,128)(2,1)S(1)} all-gather(bf16[9,512]{1,0:T(8,128)(2,1)S(1)} %pad_maximum_fusion.8), channel_id=1, replica_groups=mesh['row'=16,'col'=16] {'row'}, dimensions={1}, use_global_device_ids=true | all-gather | bytes 156672 | tf_op jit(solution)/shard_map/all_gather | solution.py:95
  44.5 4.5 fusion.15
  51.9 3.5 fusion.21
  57.2 185.2 %reduce-scatter.7.cloned.1.call-done = f32[9,512]{1,0:T(8,128)} async-done(((f32[9,8192]{1,0:T(8,128)}), f32[9,512]{1,0:T(8,128)}) %reduce-scatter.7.cloned.1.call-update) | async-done | bytes 18448 | tf_op jit(solution)/shard_map/reduce_scatter | solution.py:103
  242.5 65.7 %reduce-scatter.9.cloned.1.call-done = f32[9,512]{1,0:T(8,128)} async-done(((f32[9,8192]{1,0:T(8,128)}), f32[9,512]{1,0:T(8,128)}) %reduce-scatter.9.cloned.1.call-update) | async-done | bytes 18448 | tf_op jit(solution)/shard_map/reduce_scatter | solution.py:106
  309.1 78.9 %all-reduce.2 = (f32[8,8]{0,1:T(8,128)S(1)}, f32[8,8]{0,1:T(8,128)S(1)}) all-reduce(f32[8,8]{0,1:T(8,128)S(1)} %fusion.125, f32[8,8]{0,1:T(8,128)S(1)} %fusion.117), channel_id=1, replica_groups=mesh['row'=16,'col'=16] {'row','col'}, use_global_device_ids=true, to_apply=%region_0.1 | all-reduce | flops 128 | bytes 1024 | tf_op jit(solution)/shard_map/psum | solution.py:37
  391.5 22.5 %subtract_divide_fusion.14 = (f32[1,8]{1,0:T(1,128)S(1)}, f32[1,8]{1,0:T(1,128)S(1)}, f32[1,8]{1,0:T(1,128)S(1)}, f32[1,8]{1,0:T(1,128)S(1)}, f32[1,8]{1,0:T(1,1...) fusion(f32[]{:T(128)} %bitcast.36, f32[]{:T(128)} %bitcast.35, f32[]{:T(128)} %bitcast.34, ...), kind=kLoop, calls=%fused_computation.199 | loop fusion | flops 512 | bytes 656 | tf_op jit(solution)/shard_map/div | solution.py:19
  414.8 18.4 %all_gather.10 = bf16[8,8192]{1,0:T(8,128)(2,1)S(1)} all-gather(bf16[8,512]{1,0:T(8,128)(2,1)S(1)} %get-tuple-element.153), channel_id=1, replica_groups=mesh['row'=16,'col'=16] {'row'}, dimensions={1}, use_global_device_ids=true | all-gather | bytes 139264 | tf_op jit(solution)/shard_map/all_gather | solution.py:95
  433.9 6.0 all-to-all-start.1
  440.6 4.5 fusion.27
  449.5 3.4 fusion.33
  454.7 181.7 %reduce-scatter.11.cloned.1.call-done = f32[8,512]{1,0:T(8,128)} async-done(((f32[8,8192]{1,0:T(8,128)}), f32[8,512]{1,0:T(8,128)}) %reduce-scatter.11.cloned.1.call-update) | async-done | bytes 16400 | tf_op jit(solution)/shard_map/reduce_scatter | solution.py:103
  636.4 65.2 %reduce-scatter.13.cloned.1.call-done = f32[8,512]{1,0:T(8,128)} async-done(((f32[8,8192]{1,0:T(8,128)}), f32[8,512]{1,0:T(8,128)}) %reduce-scatter.13.cloned.1.call-update) | async-done | bytes 16400 | tf_op jit(solution)/shard_map/reduce_scatter | solution.py:106
  702.7 79.0 %all-reduce.1 = (f32[8,8]{0,1:T(8,128)S(1)}, f32[8,8]{0,1:T(8,128)S(1)}) all-reduce(f32[8,8]{0,1:T(8,128)S(1)} %fusion.182, f32[8,8]{0,1:T(8,128)S(1)} %fusion.185), channel_id=1, replica_groups=mesh['row'=16,'col'=16] {'row','col'}, use_global_device_ids=true, to_apply=%region_6.9 | all-reduce | flops 128 | bytes 1024 | tf_op jit(solution)/shard_map/psum | solution.py:37
  785.2 22.5 %subtract_divide_fusion.7 = (f32[1,8]{1,0:T(1,128)S(1)}, f32[1,8]{1,0:T(1,128)S(1)}, f32[1,8]{1,0:T(1,128)S(1)}, f32[1,8]{1,0:T(1,128)S(1)}, f32[1,8]{1,0:T(1,12...) fusion(f32[]{:T(128)} %bitcast.88, f32[]{:T(128)} %bitcast.87, f32[]{:T(128)} %bitcast.86, ...), kind=kLoop, calls=%fused_computation.190 | loop fusion | flops 512 | bytes 656 | tf_op jit(solution)/shard_map/div | solution.py:19
  808.5 18.5 %all_gather.11 = bf16[8,8192]{1,0:T(8,128)(2,1)S(1)} all-gather(bf16[8,512]{1,0:T(8,128)(2,1)S(1)} %get-tuple-element.155), channel_id=1, replica_groups=mesh['row'=16,'col'=16] {'row'}, dimensions={1}, use_global_device_ids=true | all-gather | bytes 139264 | tf_op jit(solution)/shard_map/all_gather | solution.py:95
  827.6 5.9 all-to-all-start.2
  834.3 4.5 fusion.39
  843.2 3.4 fusion.45
  848.3 181.9 %reduce-scatter.15.cloned.1.call-done = f32[8,512]{1,0:T(8,128)} async-done(((f32[8,8192]{1,0:T(8,128)}), f32[8,512]{1,0:T(8,128)}) %reduce-scatter.15.cloned.1.call-update) | async-done | bytes 16400 | tf_op jit(solution)/shard_map/reduce_scatter | solution.py:103
  1030.2 65.2 %reduce-scatter.17.cloned.1.call-done = f32[8,512]{1,0:T(8,128)} async-done(((f32[8,8192]{1,0:T(8,128)}), f32[8,512]{1,0:T(8,128)}) %reduce-scatter.17.cloned.1.call-update) | async-done | bytes 16400 | tf_op jit(solution)/shard_map/reduce_scatter | solution.py:106
  1096.4 78.9 %all-reduce = (f32[8,8]{0,1:T(8,128)S(1)}, f32[8,8]{0,1:T(8,128)S(1)}) all-reduce(f32[8,8]{0,1:T(8,128)S(1)} %fusion.188, f32[8,8]{0,1:T(8,128)S(1)} %fusion.191), channel_id=1, replica_groups=mesh['row'=16,'col'=16] {'row','col'}, use_global_device_ids=true, to_apply=%region_10.14 | all-reduce | flops 128 | bytes 1024 | tf_op jit(solution)/shard_map/psum | solution.py:37
  1178.9 22.5 %subtract_divide_fusion = (f32[1,8]{1,0:T(1,128)S(1)}, f32[1,8]{1,0:T(1,128)S(1)}, f32[1,8]{1,0:T(1,128)S(1)}, f32[1,8]{1,0:T(1,128)S(1)}, f32[1,8]{1,0:T(1,128)...) fusion(f32[]{:T(128)} %bitcast.135, f32[]{:T(128)} %bitcast.134, f32[]{:T(128)} %bitcast.133, ...), kind=kLoop, calls=%fused_computation.183 | loop fusion | flops 512 | bytes 656 | tf_op jit(solution)/shard_map/div | solution.py:19
  (123 shorter events, 40.9 us)
Async XLA Ops:
  9.3 41.5 %all-to-all-start = ((bf16[16,9,512]{2,1,0:T(8,128)(2,1)}), bf16[16,9,512]{2,1,0:T(8,128)(2,1)S(1)}, u32[]{:S(2)}, u32[]{:S(2)}) async-start(bf16[16,9,512]{2,1,0:T(8,128)(2,1)} %stack.13), calls=%async_computation.1 | async-start | bytes 524288 | tf_op jit(solution)/shard_map/all_to_all | solution.py:97
  21.1 221.4 %reduce-scatter.7.cloned.1.call-start = ((), (), s32[]{:S(2)}) async-start(), calls=%async_computation.9 | async-start | bytes 557056 | tf_op jit(solution)/shard_map/reduce_scatter | solution.py:103
  44.5 6.3 copy-start.2
  50.7 257.4 %reduce-scatter.9.cloned.1.call-start = ((), (), s32[]{:S(2)}) async-start(), calls=%async_computation.10 | async-start | bytes 557056 | tf_op jit(solution)/shard_map/reduce_scatter | solution.py:106
  51.9 5.2 copy-start.1
  51.9 5.2 copy-start
  433.9 14.9 %all-to-all-start.1 = ((bf16[16,8,512]{2,1,0:T(8,128)(2,1)}), bf16[16,8,512]{2,1,0:T(8,128)(2,1)S(1)}, u32[]{:S(2)}, u32[]{:S(2)}) async-start(bf16[16,8,512]{2,1,0:T(8,128)(2,1)} %stack.15), calls=%async_computation.4 | async-start | bytes 262144 | tf_op jit(solution)/shard_map/all_to_all | solution.py:97
  439.9 196.6 %reduce-scatter.11.cloned.1.call-start = ((), (), s32[]{:S(2)}) async-start(), calls=%async_computation.11 | async-start | bytes 278528 | tf_op jit(solution)/shard_map/reduce_scatter | solution.py:103
  446.4 255.3 %reduce-scatter.13.cloned.1.call-start = ((), (), s32[]{:S(2)}) async-start(), calls=%async_computation.12 | async-start | bytes 278528 | tf_op jit(solution)/shard_map/reduce_scatter | solution.py:106
  827.6 14.9 %all-to-all-start.2 = ((bf16[16,8,512]{2,1,0:T(8,128)(2,1)}), bf16[16,8,512]{2,1,0:T(8,128)(2,1)S(1)}, u32[]{:S(2)}, u32[]{:S(2)}) async-start(bf16[16,8,512]{2,1,0:T(8,128)(2,1)} %stack.17), calls=%async_computation.7 | async-start | bytes 262144 | tf_op jit(solution)/shard_map/all_to_all | solution.py:97
  833.5 196.6 %reduce-scatter.15.cloned.1.call-start = ((), (), s32[]{:S(2)}) async-start(), calls=%async_computation.13 | async-start | bytes 278528 | tf_op jit(solution)/shard_map/reduce_scatter | solution.py:103
  840.0 255.3 %reduce-scatter.17.cloned.1.call-start = ((), (), s32[]{:S(2)}) async-start(), calls=%async_computation.14 | async-start | bytes 278528 | tf_op jit(solution)/shard_map/reduce_scatter | solution.py:106
Sparse Core Ops, SparseCore 0:
  50.9 191.5 reduce-scatter.6
  245.1 62.9 reduce-scatter.8
  446.5 189.8 reduce-scatter.10
  638.9 62.6 reduce-scatter.12
  840.2 189.9 reduce-scatter.14
  1032.7 62.6 reduce-scatter.16
